TPU v7x, 256 devices: a whole 4x4x8 slice. The times are simulated.
256 devices in a mesh: space: 16 (over x, z_hi), snap: 16 (over y, z_lo, core).
Axes of the slice: x: 4, y: 4, z: 8 (z_hi: 4, z_lo: 2; z = z_hi * 2 + z_lo), core: 2. Of those that a mesh axis runs over, the one named last changes fastest.
Arguments:
- velocity: bfloat16 [256, 3, 128, 32, 128], P('snap', None, 'space'), may hold values from -40 to 40
- phase_bins: int32 [256], replicated, may hold values from 0 to 23, as said below
- tile_owner: int32 [16], replicated, may hold values from 0 to 15, each once
Outputs:
- gram_tiles: float32 [16, 16, 256], P('space', None, 'snap')
Inputs may be any that keep to these rules, and one draw needn't show every extreme that they name: `phase_bins`: every bin holds at least one snapshot. `tile_owner`: each tile has exactly one owner.
All inputs are finite; a program needn't handle non-finite values.
Results may differ from a plain program's by a relative error of at most 0.0003.
Values may be sent and summed in bfloat16 or wider, within the bound.
No kernel may reach another device: no remote copies, remote signals or barrier semaphores. Data moves between devices by JAX's collectives and lax.ppermute only.
A program may use at most 128 MiB of HBM per device.

v0:
```python
import jax
import jax.numpy as jnp
from jax import lax
from jax.sharding import PartitionSpec as P

NB = 24


def with_halo(block, sides, width):
    for axis, dim in sides:
        count = lax.axis_size(axis)
        forward = [(i, i + 1) for i in range(count - 1)]
        backward = [(target, source) for source, target in forward]
        low = lax.ppermute(
            lax.slice_in_dim(block, block.shape[dim] - width, None, axis=dim), axis, forward
        )
        high = lax.ppermute(lax.slice_in_dim(block, 0, width, axis=dim), axis, backward)
        block = jnp.concatenate([low, block, high], axis=dim)
    return block


def widen(field_in, direction):
    widths = [(0, 0)] * field_in.ndim
    widths[direction] = (2, 2)
    return jnp.pad(field_in, widths)


def derivative(padded_field, direction):
    length = padded_field.shape[direction] - 4

    def window_at(offset):
        return lax.slice_in_dim(padded_field, offset, offset + length, axis=direction)

    return (8.0 * (window_at(3) - window_at(1)) - (window_at(4) - window_at(0))) / 12.0


def curl_field(u_field, v_field, w_field, v_wide, w_wide, first):
    second = first + 1
    third = first + 2
    omega_x = derivative(widen(w_field, second), second) - derivative(widen(v_field, third), third)
    omega_y = derivative(widen(u_field, third), third) - derivative(w_wide, first)
    omega_z = derivative(v_wide, first) - derivative(widen(u_field, second), second)
    return jnp.stack([omega_x, omega_y, omega_z], axis=first)


def per_device(velocity, phase_bins, tile_owner):
    widened = with_halo(velocity, (("space", 2),), 2).astype(jnp.float32)
    v_wide = widened[:, 1]
    w_wide = widened[:, 2]
    frame_float = velocity.astype(jnp.float32)
    vortex = curl_field(
        frame_float[:, 0], frame_float[:, 1], frame_float[:, 2], v_wide, w_wide, 1
    ).astype(jnp.bfloat16)
    snaps_dev, _, cells_x, cells_y, cells_z = vortex.shape
    flattened = vortex.reshape(snaps_dev, 3, cells_x * cells_y * cells_z)
    arranged = lax.all_to_all(flattened, "snap", split_axis=2, concat_axis=0, tiled=True)
    total_snaps = arranged.shape[0]
    columns = arranged.reshape(total_snaps, -1)
    onehot = (phase_bins[None, :] == jnp.arange(NB, dtype=jnp.int32)[:, None]).astype(jnp.bfloat16)
    bin_counts = jnp.sum(onehot.astype(jnp.float32), axis=1)
    bin_sums = jnp.dot(onehot, columns, preferred_element_type=jnp.float32)
    bin_means = bin_sums / bin_counts[:, None]
    fluctuation = (columns.astype(jnp.float32) - jnp.take(bin_means, phase_bins, axis=0)).astype(
        jnp.bfloat16
    )
    voxel_total = lax.axis_size("space") * cells_x * cells_y * cells_z
    partial_gram = (
        lax.dot_general(
            fluctuation, fluctuation, (((1,), (1,)), ((), ())), preferred_element_type=jnp.float32
        )
        / voxel_total
    )
    tile_count = lax.axis_size("space")
    tile_ids = jnp.arange(tile_count, dtype=jnp.int32)
    inverse = jnp.sum(
        tile_ids[None, :] * (tile_owner[None, :] == tile_ids[:, None]).astype(jnp.int32), axis=1
    )
    blocks = jnp.take(
        partial_gram.reshape(tile_count, total_snaps // tile_count, total_snaps), inverse, axis=0
    )
    rows_done = lax.psum_scatter(blocks, "space", scatter_dimension=0, tiled=True)
    return lax.psum_scatter(rows_done, "snap", scatter_dimension=2, tiled=True)


def solution(mesh):
    return jax.shard_map(
        per_device,
        mesh=mesh,
        in_specs=(P("snap", None, "space", None, None), P(), P()),
        out_specs=P("space", None, "snap"),
        check_vma=False,
    )
```

profile of v0, /device:TPU:2, one launch (start us, length us, event | category | flops | bytes accessed | tf_op | source)
XLA Modules:
  0.0 431.2 jit_solution(14037773328832607324)
XLA Ops:
  6.5 0.0 slice-start
  6.5 0.0 copy-start.2
  6.5 1.1 slice-done
  7.7 1.0 copy.77
  8.6 8.2 %collective-permute-start.1 = (bf16[16,3,2,32,128]{4,3,2,0,1:T(8,128)(2,1)}, bf16[16,3,2,32,128]{4,3,2,0,1:T(8,128)(2,1)}, u32[]{:S(2)}, u32[]{:S(2)}) collective-permute-start(bf16[16,3,2,32,128]{4,3,2,0,1:T(8,128)(2,1)} %copy.77), channel_id=1, source_target_pairs={{16,0},{32,16},{48,32},{64,48},{80,64},{96,80},{112,96},{128,112},... | collective-permute-start | bytes 2359304 | tf_op jit(solution)/shard_map/ppermute | solution.py:17
  16.8 2.1 slice.108
  18.9 1.9 collective-permute-start
  20.8 0.0 copy-done.2
  20.8 0.8 convert_element_type.33
  21.7 2.4 slice_bitcast_fusion.1
  24.1 0.0 copy-start.3
  24.1 3.1 fusion.7
  27.2 2.3 stack.12
  29.5 0.0 copy-start.4
  29.5 21.3 %collective-permute-done.1 = bf16[16,3,2,32,128]{4,3,2,0,1:T(8,128)(2,1)} collective-permute-done((bf16[16,3,2,32,128]{4,3,2,0,1:T(8,128)(2,1)}, bf16[16,3,2,32,128]{4,3,2,0,1:T(8,128)(2,1)}, u32[]{:S(2)}, u32[]{:S(2)}) %collective-permute-start.1) | collective-permute-done | bytes 786464 | tf_op jit(solution)/shard_map/ppermute | solution.py:17
  50.8 8.6 %collective-permute-done = bf16[16,3,2,32,128]{4,3,2,1,0:T(8,128)(2,1)} collective-permute-done((bf16[16,3,2,32,128]{4,3,2,1,0:T(8,128)(2,1)}, bf16[16,3,2,32,128]{4,3,2,1,0:T(8,128)(2,1)}, u32[]{:S(2)}, u32[]{:S(2)}) %collective-permute-start) | collective-permute-done | bytes 786464 | tf_op jit(solution)/shard_map/ppermute | solution.py:14
  59.4 0.0 copy-done.3
  59.4 2.0 convert_bitcast_fusion
  61.4 0.0 copy-done.4
  61.4 4.2 fusion.26
  65.6 1.3 stack.13
  66.9 1.2 stack.14
  68.2 2.2 pad_maximum_fusion
  70.3 31.0 %copy.55 = bf16[16,3,32768]{0,1,2:T(4,128)(2,1)} copy(bf16[16,3,32768]{2,0,1:T(8,128)(2,1)S(1)} %pad_maximum_fusion) | data formatting | bytes 6291456 | tf_op jit(solution)/shard_map/stack | solution.py:43
  101.3 29.5 %reshape.77 = bf16[16,2,49152]{2,1,0:T(2,128)(2,1)} reshape(bf16[32768,3,16]{2,1,0:T(4,128)(2,1)} %bitcast.45) | data formatting | bytes 6291456
  130.8 0.0 copy-start.5
  130.8 0.0 copy-start.6
  130.8 5.7 %all-to-all-start = ((bf16[16,2,49152]{2,1,0:T(2,128)(2,1)}), bf16[16,2,49152]{2,1,0:T(2,128)(2,1)S(1)}, u32[]{:S(2)}, u32[]{:S(2)}) async-start(bf16[16,2,49152]{2,1,0:T(2,128)(2,1)} %reshape.77), calls=%async_computation | async-start | bytes 6291456 | tf_op jit(solution)/shard_map/all_to_all | solution.py:56
  136.5 0.0 reduce-scatter.5.cloned.1.call-start
  136.6 0.0 copy-done.5
  136.6 0.1 broadcast_in_dim.31
  136.7 0.1 copy.57
  136.8 0.0 copy-done.6
  136.8 0.1 select_reduce_fusion
  137.0 0.1 convert_reduce_fusion
  137.1 38.5 %all-to-all-done = bf16[16,2,49152]{2,1,0:T(2,128)(2,1)S(1)} async-done(((bf16[16,2,49152]{2,1,0:T(2,128)(2,1)}), bf16[16,2,49152]{2,1,0:T(2,128)(2,1)S(1)}, u32[]{:S(2)}, u32[]{:S(2)}) %all-to-all-start) | async-done | bytes 3145760 | tf_op jit(solution)/shard_map/all_to_all | solution.py:56
  175.6 32.7 %reshape.78 = bf16[32768,3,16]{2,1,0:T(4,128)(2,1)} reshape(bf16[16,2,49152]{2,1,0:T(2,128)(2,1)S(1)} %all-to-all-done) | data formatting | bytes 6291456
  208.3 30.1 %copy.61 = bf16[16,3,16,2048]{3,2,0,1:T(8,128)(2,1)S(1)} copy(bf16[16,3,16,2048]{0,1,3,2:T(4,128)(2,1)} %bitcast.46) | data formatting | bytes 6291456 | tf_op jit(solution)/shard_map/all_to_all | solution.py:56
  238.4 0.0 copy-start
  238.4 2.7 copy.58
  241.1 0.0 copy-done
  241.1 3.3 copy.66
  244.5 0.5 convolution_divide_fusion
  245.0 5.2 %gather_fusion = f32[256,6144]{1,0:T(8,128)} fusion(f32[24,6144]{1,0:T(8,128)S(1)} %convolution_divide_fusion, s32[1024]{0:T(1024)S(1)} %pad_clamp_fusion.1), kind=kCustom, calls=%fused_computation | custom fusion | bytes 12583936 | tf_op jit(solution)/shard_map/jit(_take)/gather | solution.py:63
  250.2 0.0 copy-start.1
  250.2 11.5 %gather.11 = f32[16,16,3,2048]{3,2,1,0:T(4,128)} reshape(f32[256,6144]{1,0:T(8,128)} %gather_fusion) | data formatting | bytes 12582912 | tf_op jit(solution)/shard_map/jit(_take)/gather | solution.py:63
  261.7 0.0 copy-done.1
  261.7 7.4 %fusion.1 = bf16[16,16,3,2048]{3,0,1,2:T(8,128)(2,1)S(1)} fusion(f32[16,16,3,2048]{3,2,1,0:T(4,128)} %gather.11, pred[16,16]{0,1:T(8,128)(4,1)S(1)} %copy.57, bf16[16,3,16,2048]{3,2,0,1:T(8,128)(2,1)S(1)} %copy-done.1), kind=kLoop, calls=%fused_computation.13 | loop fusion | flops 6291456 | bytes 12583168 | tf_op jit(solution)/shard_map/convert_element_type | solution.py:63
  269.1 2.7 copy.60
  271.8 3.3 copy.67
  275.1 1.0 convolution_multiply_fusion
  276.1 0.6 gather_fusion.1
  276.7 0.8 broadcast_select_fusion
  277.5 0.0 reduce-scatter.5.cloned.1.call-update
  277.5 0.0 reduce-scatter.7.cloned.1.call-start
  277.6 80.9 %reduce-scatter.5.cloned.1.call-done = f32[1,16,256]{2,1,0:T(8,128)} async-done(((f32[16,16,256]{2,1,0:T(8,128)}), f32[1,16,256]{2,1,0:T(8,128)}) %reduce-scatter.5.cloned.1.call-update) | async-done | bytes 16400 | tf_op jit(solution)/shard_map/reduce_scatter | solution.py:81
  358.5 1.5 copy.62
  359.9 0.0 reduce-scatter.7.cloned.1.call-update
  360.0 63.0 %reduce-scatter.7.cloned.1.call-done = f32[16,16]{1,0:T(8,128)} async-done(((f32[256,16]{1,0:T(8,128)}), f32[16,16]{1,0:T(8,128)}) %reduce-scatter.7.cloned.1.call-update) | async-done | bytes 1040
  423.0 1.4 copy.63
  (6 shorter events, 0.0 us)
Async XLA Ops:
  6.5 1.1 slice-start
  6.5 14.3 %copy-start.2 = (bf16[16,3,8,32,128]{4,3,2,1,0:T(8,128)(2,1)S(1)}, bf16[16,3,8,32,128]{4,3,2,1,0:T(8,128)(2,1)}, u32[]{:S(2)}) copy-start(bf16[16,3,8,32,128]{4,3,2,1,0:T(8,128)(2,1)} %param.3) | copy-start | bytes 9437188
  8.6 42.2 %collective-permute-start.1 = (bf16[16,3,2,32,128]{4,3,2,0,1:T(8,128)(2,1)}, bf16[16,3,2,32,128]{4,3,2,0,1:T(8,128)(2,1)}, u32[]{:S(2)}, u32[]{:S(2)}) collective-permute-start(bf16[16,3,2,32,128]{4,3,2,0,1:T(8,128)(2,1)} %copy.77), channel_id=1, source_target_pairs={{16,0},{32,16},{48,32},{64,48},{80,64},{96,80},{112,96},{128,112},... | collective-permute-start | bytes 2359304 | tf_op jit(solution)/shard_map/ppermute | solution.py:17
  18.9 40.5 %collective-permute-start = (bf16[16,3,2,32,128]{4,3,2,1,0:T(8,128)(2,1)}, bf16[16,3,2,32,128]{4,3,2,1,0:T(8,128)(2,1)}, u32[]{:S(2)}, u32[]{:S(2)}) collective-permute-start(bf16[16,3,2,32,128]{4,3,2,1,0:T(8,128)(2,1)} %slice.108), channel_id=1, source_target_pairs={{0,16},{16,32},{32,48},{48,64},{64,80},{80,96},{96,112},{112,128},... | collective-permute-start | bytes 2359304 | tf_op jit(solution)/shard_map/ppermute | solution.py:14
  24.1 35.3 %copy-start.3 = (bf16[16,3,8,32,128]{4,3,2,1,0:T(8,128)(2,1)S(1)}, bf16[16,3,8,32,128]{4,3,2,1,0:T(8,128)(2,1)}, u32[]{:S(2)}) copy-start(bf16[16,3,8,32,128]{4,3,2,1,0:T(8,128)(2,1)} %param.3) | copy-start | bytes 9437188
  29.5 31.9 %copy-start.4 = (f32[16,8,32,128]{3,2,1,0:T(8,128)S(1)}, f32[16,8,32,128]{3,2,1,0:T(8,128)}, u32[]{:S(2)}) copy-start(f32[16,8,32,128]{3,2,1,0:T(8,128)} %get-tuple-element.7) | copy-start | bytes 6291460
  130.8 5.8 %copy-start.5 = (s32[256]{0:T(256)S(1)}, s32[256]{0:T(256)}, u32[]{:S(2)}) copy-start(s32[256]{0:T(256)} %param.4) | copy-start | bytes 3076
  130.8 6.0 %copy-start.6 = (s32[16]{0:T(128)S(1)}, s32[16]{0:T(128)}, u32[]{:S(2)}) copy-start(s32[16]{0:T(128)} %param.5) | copy-start | bytes 196
  130.8 44.8 %all-to-all-start = ((bf16[16,2,49152]{2,1,0:T(2,128)(2,1)}), bf16[16,2,49152]{2,1,0:T(2,128)(2,1)S(1)}, u32[]{:S(2)}, u32[]{:S(2)}) async-start(bf16[16,2,49152]{2,1,0:T(2,128)(2,1)} %reshape.77), calls=%async_computation | async-start | bytes 6291456 | tf_op jit(solution)/shard_map/all_to_all | solution.py:56
  136.5 221.9 %reduce-scatter.5.cloned.1.call-start = ((), (), s32[]{:S(2)}) async-start(), calls=%async_computation.3 | async-start | bytes 278528 | tf_op jit(solution)/shard_map/reduce_scatter | solution.py:81
  238.4 2.7 copy-start
  250.2 11.5 %copy-start.1 = (bf16[16,3,16,2048]{3,2,0,1:T(8,128)(2,1)S(1)}, bf16[16,3,16,2048]{3,2,0,1:T(8,128)(2,1)}, u32[]{:S(2)}) copy-start(bf16[16,3,16,2048]{3,2,0,1:T(8,128)(2,1)} %copy-done) | copy-start | bytes 9437188
  277.5 145.5 %reduce-scatter.7.cloned.1.call-start = ((), (), s32[]{:S(2)}) async-start(), calls=%async_computation.4 | async-start | bytes 139264
Sparse Core Ops, SparseCore 0:
  277.6 80.8 reduce-scatter.4
  361.0 61.9 reduce-scatter.6
where the time goes:
time: 433 us; the launch traced here: 431 us
  waiting for transfers between devices  212 us (49%)
  local copies, waits for them, and re-layouts  167 us (39%)
  other arithmetic  20.8 us (5%)
  starting transfers between devices  15.9 us (4%)
  between operations  13.6 us (3%)
    reduce_scatter x1, waiting for transfers between devices, per_device(): lax.psum_scatter(blocks, 'space', scatter_dimension=0, tiled=True)  80.9 us
    unnamed x21, local copies, waits for them, and re-layouts  72.7 us
    unnamed x3, waiting for transfers between devices  63 us
    all_to_all x1, waiting for transfers between devices, per_device(): lax.all_to_all(flattened, 'snap', split_axis=2, concat_axis=0, tiled=True)  38.5 us
    another operation x4, local copies, waits for them, and re-layouts, curl_field(): return jnp.stack([omega_x, omega_y, omega_z], axis=first)  35.8 us
    all_to_all x2, local copies, waits for them, and re-layouts, per_device(): lax.all_to_all(flattened, 'snap', split_axis=2, concat_axis=0, tiled=True)  32.8 us
    ppermute x1, waiting for transfers between devices, with_halo(): lax.ppermute(lax.slice_in_dim(block, 0, width, axis=dim), axis, backward)  21.3 us
    gather x2, local copies, waits for them, and re-layouts, per_device(): jnp.take(bin_means, phase_bins, axis=0)  16.7 us
  transfers between devices with their start and end apart: 5, of which 5 were waited for; matrix products, arithmetic and copies ran while one was open for 3% of the time, Pallas kernels for 0%

commit v1 on v0

--- a/solution.py
+++ b/solution.py
@@ -53,7 +53,12 @@
     ).astype(jnp.bfloat16)
     snaps_dev, _, cells_x, cells_y, cells_z = vortex.shape
     flattened = vortex.reshape(snaps_dev, 3, cells_x * cells_y * cells_z)
-    arranged = lax.all_to_all(flattened, "snap", split_axis=2, concat_axis=0, tiled=True)
+    arranged = jnp.concatenate(
+        lax.all_to_all(
+            jnp.stack(jnp.split(flattened, lax.axis_size("snap"), axis=2)), "snap", 0, 0
+        ),
+        axis=0,
+    )
     total_snaps = arranged.shape[0]
     columns = arranged.reshape(total_snaps, -1)
     onehot = (phase_bins[None, :] == jnp.arange(NB, dtype=jnp.int32)[:, None]).astype(jnp.bfloat16)

time: 433 us -> 325 us (0.75)
  local copies, waits for them, and re-layouts: 167 us -> 62.1 us
    unnamed x21 -> x36, local copies, waits for them, and re-layouts: 72.7 us -> 24.3 us
    all_to_all x2 -> x1, local copies, waits for them, and re-layouts: 32.8 us -> 2.75 us  [per_device(): lax.all_to_all(jnp.stack(jnp.split(flattened, lax.axis_size('snap'), axis...]
    another operation x4, local copies, waits for them, and re-layouts: 35.8 us -> 8.29 us  [curl_field(): return jnp.stack([omega_x, omega_y, omega_z], axis=first)]
    another operation x3 -> x2, other arithmetic: 9.54 us -> 8.11 us
  transfers between devices with their start and end apart: 5 -> 5, of which waited for: 5 -> 5; matrix products, arithmetic and copies ran while one was open for 3% -> 4% of each run, Pallas kernels for 0% -> 0%
where the time goes in v1:
time: 325 us; the launch traced here: 324 us
  waiting for transfers between devices  210 us (65%)
  local copies, waits for them, and re-layouts  62.1 us (19%)
  other arithmetic  20.7 us (6%)
  starting transfers between devices  16.1 us (5%)
  between operations  13.6 us (4%)
    reduce_scatter x1, waiting for transfers between devices, per_device(): lax.psum_scatter(blocks, 'space', scatter_dimension=0, tiled=True)  80.9 us
    unnamed x3, waiting for transfers between devices  62.8 us
    all_to_all x1, waiting for transfers between devices, per_device(): lax.all_to_all(jnp.stack(jnp.split(flattened, lax.axis_size('snap'), axis...  38.4 us
    unnamed x36, local copies, waits for them, and re-layouts  24.3 us
    ppermute x1, waiting for transfers between devices, with_halo(): lax.ppermute(lax.slice_in_dim(block, 0, width, axis=dim), axis, backward)  19 us
    gather x2, local copies, waits for them, and re-layouts, per_device(): jnp.take(bin_means, phase_bins, axis=0)  16.7 us
    convert_element_type x1, other arithmetic, per_device(): (columns.astype(jnp.float32) - jnp.take(bin_means, phase_bins, axis=0)).a...  8.68 us
    ppermute x1, waiting for transfers between devices, with_halo(): lax.ppermute(lax.slice_in_dim(block, block.shape[dim] - width, None, axis...  8.66 us
  transfers between devices with their start and end apart: 5, of which 5 were waited for; matrix products, arithmetic and copies ran while one was open for 4% of the time, Pallas kernels for 0%

profile of v1, /device:TPU:2, one launch (start us, length us, event | category | flops | bytes accessed | tf_op | source)
XLA Modules:
  0.0 323.8 jit_solution(7885252272439903787)
XLA Ops:
  6.5 1.3 slice.131
  7.9 0.9 copy.56
  8.8 8.2 %collective-permute-start.1 = (bf16[16,3,2,32,128]{4,3,2,0,1:T(8,128)(2,1)}, bf16[16,3,2,32,128]{4,3,2,0,1:T(8,128)(2,1)}, u32[]{:S(2)}, u32[]{:S(2)}) collective-permute-start(bf16[16,3,2,32,128]{4,3,2,0,1:T(8,128)(2,1)} %copy.56), channel_id=1, source_target_pairs={{16,0},{32,16},{48,32},{64,48},{80,64},{96,80},{112,96},{128,112},... | collective-permute-start | bytes 2359304 | tf_op jit(solution)/shard_map/ppermute | solution.py:17
  17.0 2.2 slice.108
  19.2 1.9 collective-permute-start
  21.1 0.0 copy-done.2
  21.1 0.8 convert_element_type.33
  21.9 2.4 slice_bitcast_fusion
  24.3 3.1 fusion.7
  27.4 2.3 stack.63
  29.7 2.3 constant_dynamic-update-slice_fusion.2
  32.0 19.0 %collective-permute-done.1 = bf16[16,3,2,32,128]{4,3,2,0,1:T(8,128)(2,1)} collective-permute-done((bf16[16,3,2,32,128]{4,3,2,0,1:T(8,128)(2,1)}, bf16[16,3,2,32,128]{4,3,2,0,1:T(8,128)(2,1)}, u32[]{:S(2)}, u32[]{:S(2)}) %collective-permute-start.1) | collective-permute-done | bytes 786464 | tf_op jit(solution)/shard_map/ppermute | solution.py:17
  51.0 8.7 %collective-permute-done = bf16[16,3,2,32,128]{4,3,2,1,0:T(8,128)(2,1)} collective-permute-done((bf16[16,3,2,32,128]{4,3,2,1,0:T(8,128)(2,1)}, bf16[16,3,2,32,128]{4,3,2,1,0:T(8,128)(2,1)}, u32[]{:S(2)}, u32[]{:S(2)}) %collective-permute-start) | collective-permute-done | bytes 786464 | tf_op jit(solution)/shard_map/ppermute | solution.py:14
  59.6 2.0 convert_bitcast_fusion.1
  61.6 0.0 copy-done.3
  61.7 5.0 %fusion.14 = (bf16[16,8,32,128]{3,2,1,0:T(8,128)(2,1)}, bf16[16,8,32,128]{3,2,1,0:T(8,128)(2,1)}) fusion(f32[16,8,32,128]{3,2,1,0:T(8,128)S(1)} %copy-done.3, f32[16,12,32,128]{3,2,1,0:T(8,128)S(1)} %get-tuple-element.8, f32[16,12,32,128]{3,2,1,0:T(8,128)S(1)} %get-tuple-element.9), kind=kLoop, calls=%fused_computation.36 | loop fusion | flops 12582912 | bytes 20971520 | tf_op jit(solution)/shard_map/convert.3
  66.7 2.4 stack.64
  69.1 2.3 stack.65
  71.4 0.0 copy-done.4
  71.4 1.3 constant_dynamic-update-slice_fusion.1
  72.7 1.3 constant_dynamic-update-slice_fusion
  74.0 0.7 fusion.49
  74.7 0.7 fusion.48
  75.3 0.7 fusion.47
  76.0 0.7 fusion.46
  76.7 0.7 fusion.45
  77.4 0.7 fusion.44
  78.1 0.7 fusion.43
  78.8 0.7 fusion.42
  79.5 0.7 fusion.41
  80.2 0.7 fusion.40
  80.9 0.7 fusion.39
  81.6 0.7 fusion.38
  82.2 0.7 fusion.37
  82.9 0.7 fusion.36
  83.6 0.7 fusion.35
  84.3 0.7 fusion.34
  85.0 5.7 %all-to-all-start = ((bf16[16,16,3,2048]{3,1,2,0:T(8,128)(2,1)}), bf16[16,16,3,2048]{3,1,2,0:T(8,128)(2,1)S(1)}, u32[]{:S(2)}, u32[]{:S(2)}) async-start(bf16[16,16,3,2048]{3,1,2,0:T(8,128)(2,1)} %fusion.34), calls=%async_computation | async-start | bytes 6291456 | tf_op jit(solution)/shard_map/all_to_all | solution.py:57
  90.8 0.2 reduce-scatter.5.cloned.1.call-start
  91.0 0.0 copy-done.5
  91.1 0.1 broadcast_in_dim.31
  91.1 0.0 copy-done.6
  91.1 0.1 select_reduce_fusion
  91.3 0.1 convert_reduce_fusion
  91.4 38.4 %all-to-all-done = bf16[16,16,3,2048]{3,1,2,0:T(8,128)(2,1)S(1)} async-done(((bf16[16,16,3,2048]{3,1,2,0:T(8,128)(2,1)}), bf16[16,16,3,2048]{3,1,2,0:T(8,128)(2,1)S(1)}, u32[]{:S(2)}, u32[]{:S(2)}) %all-to-all-start) | async-done | bytes 3145760 | tf_op jit(solution)/shard_map/all_to_all | solution.py:57
  129.9 2.8 copy.38
  132.6 0.0 copy-done
  132.6 3.3 %copy.45 = bf16[32,8,3,2048]{3,1,2,0:T(8,128)(2,1)S(1)} copy(bf16[32,8,3,2048]{3,2,1,0:T(4,128)(2,1)S(1)} %bitcast.105) | data formatting | bytes 6291456
  135.9 0.5 convolution_divide_fusion
  136.5 5.2 %gather_fusion = f32[256,6144]{1,0:T(8,128)} fusion(f32[24,6144]{1,0:T(8,128)S(1)} %convolution_divide_fusion, s32[1024]{0:T(1024)S(1)} %get-tuple-element.13), kind=kCustom, calls=%fused_computation | custom fusion | bytes 12583936 | tf_op jit(solution)/shard_map/jit(_take)/gather | solution.py:68
  141.7 11.5 %gather.11 = f32[16,16,3,2048]{3,2,1,0:T(4,128)} reshape(f32[256,6144]{1,0:T(8,128)} %gather_fusion) | data formatting | bytes 12582912 | tf_op jit(solution)/shard_map/jit(_take)/gather | solution.py:68
  153.2 8.7 %fusion.1 = bf16[16,16,3,2048]{3,1,2,0:T(8,128)(2,1)S(1)} fusion(f32[16,16,3,2048]{3,2,1,0:T(4,128)} %gather.11, bf16[16,16,3,2048]{3,1,2,0:T(8,128)(2,1)S(1)} %copy-done.1, pred[16,16]{1,0:T(8,128)(4,1)S(1)} %broadcast_in_dim.31), kind=kLoop, calls=%fused_computation.13 | loop fusion | flops 6291456 | bytes 12583168 | tf_op jit(solution)/shard_map/convert_element_type | solution.py:68
  161.8 2.8 copy.40
  164.6 3.3 %copy.46 = bf16[32,8,3,2048]{3,1,2,0:T(8,128)(2,1)S(1)} copy(bf16[32,8,3,2048]{3,2,1,0:T(4,128)(2,1)S(1)} %bitcast.104) | data formatting | bytes 6291456
  167.9 1.0 convolution_multiply_fusion
  169.0 0.6 gather_fusion.1
  169.5 0.8 broadcast_select_fusion
  170.3 0.0 reduce-scatter.5.cloned.1.call-update
  170.3 0.0 reduce-scatter.7.cloned.1.call-start
  170.4 80.9 %reduce-scatter.5.cloned.1.call-done = f32[1,16,256]{2,1,0:T(8,128)} async-done(((f32[16,16,256]{2,1,0:T(8,128)}), f32[1,16,256]{2,1,0:T(8,128)}) %reduce-scatter.5.cloned.1.call-update) | async-done | bytes 16400 | tf_op jit(solution)/shard_map/reduce_scatter | solution.py:86
  251.3 1.5 copy.41
  252.7 0.0 reduce-scatter.7.cloned.1.call-update
  252.7 62.8 %reduce-scatter.7.cloned.1.call-done = f32[16,16]{1,0:T(8,128)} async-done(((f32[256,16]{1,0:T(8,128)}), f32[16,16]{1,0:T(8,128)}) %reduce-scatter.7.cloned.1.call-update) | async-done | bytes 1040
  315.6 1.4 copy.42
  (13 shorter events, 0.0 us)
Async XLA Ops:
  6.5 14.6 %copy-start.2 = (bf16[16,3,8,32,128]{4,3,2,1,0:T(8,128)(2,1)S(1)}, bf16[16,3,8,32,128]{4,3,2,1,0:T(8,128)(2,1)}, u32[]{:S(2)}) copy-start(bf16[16,3,8,32,128]{4,3,2,1,0:T(8,128)(2,1)} %param.3) | copy-start | bytes 9437188
  8.8 42.2 %collective-permute-start.1 = (bf16[16,3,2,32,128]{4,3,2,0,1:T(8,128)(2,1)}, bf16[16,3,2,32,128]{4,3,2,0,1:T(8,128)(2,1)}, u32[]{:S(2)}, u32[]{:S(2)}) collective-permute-start(bf16[16,3,2,32,128]{4,3,2,0,1:T(8,128)(2,1)} %copy.56), channel_id=1, source_target_pairs={{16,0},{32,16},{48,32},{64,48},{80,64},{96,80},{112,96},{128,112},... | collective-permute-start | bytes 2359304 | tf_op jit(solution)/shard_map/ppermute | solution.py:17
  19.2 40.5 %collective-permute-start = (bf16[16,3,2,32,128]{4,3,2,1,0:T(8,128)(2,1)}, bf16[16,3,2,32,128]{4,3,2,1,0:T(8,128)(2,1)}, u32[]{:S(2)}, u32[]{:S(2)}) collective-permute-start(bf16[16,3,2,32,128]{4,3,2,1,0:T(8,128)(2,1)} %slice.108), channel_id=1, source_target_pairs={{0,16},{16,32},{32,48},{48,64},{64,80},{80,96},{96,112},{112,128},... | collective-permute-start | bytes 2359304 | tf_op jit(solution)/shard_map/ppermute | solution.py:14
  32.0 29.7 %copy-start.3 = (f32[16,8,32,128]{3,2,1,0:T(8,128)S(1)}, f32[16,8,32,128]{3,2,1,0:T(8,128)}, u32[]{:S(2)}) copy-start(f32[16,8,32,128]{3,2,1,0:T(8,128)} %get-tuple-element.5) | copy-start | bytes 6291460
  66.6 4.7 %copy-start.4 = (bf16[16,3,32768]{2,0,1:T(8,128)(2,1)S(1)}, bf16[16,3,32768]{2,0,1:T(8,128)(2,1)}, u32[]{:S(2)}) copy-start(bf16[16,3,32768]{2,0,1:T(8,128)(2,1)} %constant_dynamic-update-slice_fusion.2) | copy-start | bytes 9437188
  85.0 6.0 %copy-start.5 = (s32[256]{0:T(256)S(1)}, s32[256]{0:T(256)}, u32[]{:S(2)}) copy-start(s32[256]{0:T(256)} %param.4) | copy-start | bytes 3076
  85.0 6.1 %copy-start.6 = (s32[16]{0:T(128)S(1)}, s32[16]{0:T(128)}, u32[]{:S(2)}) copy-start(s32[16]{0:T(128)} %param.5) | copy-start | bytes 196
  85.0 44.8 %all-to-all-start = ((bf16[16,16,3,2048]{3,1,2,0:T(8,128)(2,1)}), bf16[16,16,3,2048]{3,1,2,0:T(8,128)(2,1)S(1)}, u32[]{:S(2)}, u32[]{:S(2)}) async-start(bf16[16,16,3,2048]{3,1,2,0:T(8,128)(2,1)} %fusion.34), calls=%async_computation | async-start | bytes 6291456 | tf_op jit(solution)/shard_map/all_to_all | solution.py:57
  90.8 160.5 %reduce-scatter.5.cloned.1.call-start = ((), (), s32[]{:S(2)}) async-start(), calls=%async_computation.3 | async-start | bytes 278528 | tf_op jit(solution)/shard_map/reduce_scatter | solution.py:86
  129.8 2.8 copy-start
  141.7 11.5 %copy-start.1 = (bf16[16,16,3,2048]{3,1,2,0:T(8,128)(2,1)S(1)}, bf16[16,16,3,2048]{3,1,2,0:T(8,128)(2,1)}, u32[]{:S(2)}) copy-start(bf16[16,16,3,2048]{3,1,2,0:T(8,128)(2,1)} %copy-done) | copy-start | bytes 9437188
  170.3 145.2 %reduce-scatter.7.cloned.1.call-start = ((), (), s32[]{:S(2)}) async-start(), calls=%async_computation.4 | async-start | bytes 139264
Sparse Core Ops, SparseCore 0:
  170.5 80.7 reduce-scatter.4
  253.7 61.7 reduce-scatter.6
